TPU v7x, 32 devices: a whole 2x2x4 slice. The times are simulated.
32 devices in a mesh: req: 8 (over y, x, core), hid: 4 (over z).
Axes of the slice: x: 2, y: 2, z: 4, core: 2. Of those that a mesh axis runs over, the one named last changes fastest.
Arguments:
- hidden_in: bfloat16 [2048, 1024], P('req', 'hid'), may hold values from -6 to 6
- segments: int32 [8, 256], P('req'), may hold values from 0 to 7, never falling along the last dimension, each value on 1 to 128 neighbouring positions
- prefix_group: int32 [8, 8], P('req'), may hold values from 0 to 15
- prefix_cache: bfloat16 [16, 1024, 8, 128], P('req', None, 'hid'), may hold values from -400 to 400
- page_table: int32 [8, 2], P('req'), may hold values from 0 to 1, each once within a row
- norm_gain: float32 [1024], replicated, may hold values from 0.1 to 1.9
- w_query: bfloat16 [1024, 1024], P(None, 'hid'), may hold values from -0.1875 to 0.1875
- w_keyval: bfloat16 [1024, 1024], P(None, 'hid'), may hold values from -0.1875 to 0.1875
- w_out: bfloat16 [1024, 1024], P('hid'), may hold values from -0.1875 to 0.1875
- moe_gain: float32 [1024], replicated, may hold values from 0.1 to 1.9
- routes: int32 [2048, 8], P('req'), may hold values from 0 to 15, all different within a row; in each aligned block of 256 rows (0 to 255, 256 to 511, ...) at most 256 rows name the same one
- gates: float32 [2048, 8], P('req'), may hold values from 0.05 to 0.5
- w_gate_up: bfloat16 [16, 2, 1024, 512], P('req', None, None, 'hid'), may hold values from -0.1875 to 0.1875
- w_down: bfloat16 [16, 512, 1024], P('req', 'hid'), may hold values from -0.25 to 0.25
Outputs:
- hidden_out: bfloat16 [2048, 1024], P('req', 'hid')
- kv_pages: bfloat16 [16, 128, 8, 128], P('req', None, 'hid')
Inputs may be any that keep to these rules, and one draw needn't show every extreme that they name: `routes`: within the 256 rows of one row of the stream no expert is named by more than 256 tokens. `page_table`: each row is a permutation of 0 to 1. `segments`: segment numbers of a row never fall; each of the 8 documents has 1 to 128 tokens.
All inputs are finite; a program needn't handle non-finite values.
Results may differ from a plain program's by a relative error of at most 0.013.
Values may be sent and summed in bfloat16 or wider, within the bound.
No kernel may reach another device: no remote copies, remote signals or barrier semaphores. Data moves between devices by JAX's collectives and lax.ppermute only.
A program may use at most 128 MiB of HBM per device.

v0:
```python
import jax
import jax.numpy as jnp
from jax import lax
from jax.sharding import PartitionSpec as P

PAGE = 128
EPSILON = 1e-06
THETA = 10000.0


def rms_scale(row_data, gain_row):
    floats = row_data.astype(jnp.float32)
    mean_square = jnp.mean(floats * floats, axis=-1, keepdims=True)
    return (floats * lax.rsqrt(mean_square + EPSILON) * gain_row).astype(jnp.bfloat16)


def rotate(features, positions):
    half_dim = features.shape[-1] // 2
    frequency = THETA ** (-2.0 * jnp.arange(half_dim, dtype=jnp.float32) / features.shape[-1])
    angles = positions.astype(jnp.float32)[:, None] * frequency[None, :]
    cosine = jnp.cos(angles)[:, None, :]
    sine_part = jnp.sin(angles)[:, None, :]
    front_half = features[..., :half_dim]
    second = features[..., half_dim:]
    return jnp.concatenate(
        [front_half * cosine - second * sine_part, second * cosine + front_half * sine_part],
        axis=-1,
    )


def positions_of(segment_row, offset):
    earlier = jnp.sum((segment_row[None, :] < segment_row[:, None]).astype(jnp.int32), axis=1)
    token_index = jnp.arange(segment_row.shape[0], dtype=jnp.int32)
    return token_index - earlier + offset


def slots_of(route_rows, experts):
    flat_routes = route_rows.reshape(-1)
    onehot = (flat_routes[:, None] == jnp.arange(experts, dtype=jnp.int32)[None, :]).astype(
        jnp.int32
    )
    before = jnp.cumsum(onehot, axis=0) - onehot
    return (flat_routes, jnp.sum(before * onehot, axis=1))


def expert_rows(received, gate_up, down_proj):
    local_experts = down_proj.shape[0]
    slot_count = received.shape[1]
    model_width = received.shape[2]
    grouped = received.reshape(-1, local_experts, slot_count, model_width)
    gate_proj = jnp.einsum(
        "recd,edf->recf", grouped, gate_up[:, 0], preferred_element_type=jnp.float32
    )
    up_proj = jnp.einsum(
        "recd,edf->recf", grouped, gate_up[:, 1], preferred_element_type=jnp.float32
    )
    hidden = (jax.nn.silu(gate_proj) * up_proj).astype(jnp.bfloat16)
    produced = jnp.einsum("recf,efd->recd", hidden, down_proj, preferred_element_type=jnp.float32)
    return produced.reshape(-1, slot_count, model_width)


def shards(
    hidden_in,
    segments,
    prefix_group,
    prefix_cache,
    page_table,
    norm_gain,
    w_query,
    w_keyval,
    w_out,
    moe_gain,
    routes,
    gates,
    w_gate_up,
    w_down,
):
    req_count = lax.axis_size("req")
    whole = lax.all_gather(hidden_in, "hid", axis=1, tiled=True)
    tok_count = whole.shape[0]
    model_width = whole.shape[1]
    segment_row = segments[0]
    prefix_len = prefix_cache.shape[1]
    kv_heads = prefix_cache.shape[2]
    head_dim = prefix_cache.shape[3] // 2
    score_scale = head_dim ** (-0.5)
    normed = rms_scale(whole, norm_gain)
    position = positions_of(segment_row, prefix_len)
    projected = jnp.dot(normed, w_query, preferred_element_type=jnp.float32).reshape(
        tok_count, -1, head_dim
    )
    queries = rotate(projected, position).astype(jnp.bfloat16)
    q_groups = queries.shape[1] // kv_heads
    grouped_query = queries.reshape(tok_count, kv_heads, q_groups, head_dim)
    key_value = jnp.dot(normed, w_keyval, preferred_element_type=jnp.float32).reshape(
        tok_count, kv_heads, 2 * head_dim
    )
    key_rows = rotate(key_value[..., :head_dim], position).astype(jnp.bfloat16)
    value_rows = key_value[..., head_dim:].astype(jnp.bfloat16)
    pages = jnp.concatenate([key_rows, value_rows], axis=-1).reshape(
        -1, PAGE, kv_heads, 2 * head_dim
    )
    kv_pages = jnp.zeros_like(pages).at[page_table[0]].set(pages)
    token_index = jnp.arange(tok_count, dtype=jnp.int32)
    visible = (segment_row[None, :] == segment_row[:, None]) & (
        token_index[None, :] <= token_index[:, None]
    )
    local_scores = (
        jnp.einsum("tkgd,skd->kgts", grouped_query, key_rows, preferred_element_type=jnp.float32)
        * score_scale
    )
    local_scores = jnp.where(visible[None, None], local_scores, -jnp.inf)
    row_max = jnp.max(local_scores, axis=-1)
    numerators = jnp.exp(local_scores - row_max[..., None])
    totals = jnp.sum(numerators, axis=-1)
    weighted = jnp.einsum(
        "kgts,skd->kgtd",
        numerators.astype(jnp.bfloat16),
        value_rows,
        preferred_element_type=jnp.float32,
    )
    gathered = lax.all_gather(prefix_cache, "req", axis=0, tiled=True)
    window = tok_count // 2
    seg_count = prefix_group.shape[1]
    for seg in range(seg_count):
        start_row = jnp.minimum(jnp.sum((segment_row < seg).astype(jnp.int32)), tok_count - window)
        chosen = lax.dynamic_index_in_dim(gathered, prefix_group[0, seg], 0, keepdims=False)
        query_window = lax.dynamic_slice_in_dim(grouped_query, start_row, window, 0)
        scores = (
            jnp.einsum(
                "tkgd,skd->kgts",
                query_window,
                chosen[..., :head_dim],
                preferred_element_type=jnp.float32,
            )
            * score_scale
        )
        old_max = lax.dynamic_slice_in_dim(row_max, start_row, window, 2)
        old_total = lax.dynamic_slice_in_dim(totals, start_row, window, 2)
        old_weighted = lax.dynamic_slice_in_dim(weighted, start_row, window, 2)
        new_max = jnp.maximum(old_max, jnp.max(scores, axis=-1))
        decay_factor = jnp.exp(old_max - new_max)
        fresh = jnp.exp(scores - new_max[..., None])
        added = jnp.einsum(
            "kgts,skd->kgtd",
            fresh.astype(jnp.bfloat16),
            chosen[..., head_dim:],
            preferred_element_type=jnp.float32,
        )
        new_total = old_total * decay_factor + jnp.sum(fresh, axis=-1)
        new_weighted = old_weighted * decay_factor[..., None] + added
        inside = lax.dynamic_slice_in_dim(segment_row, start_row, window, 0) == seg
        row_max = lax.dynamic_update_slice_in_dim(
            row_max, jnp.where(inside[None, None], new_max, old_max), start_row, 2
        )
        totals = lax.dynamic_update_slice_in_dim(
            totals, jnp.where(inside[None, None], new_total, old_total), start_row, 2
        )
        weighted = lax.dynamic_update_slice_in_dim(
            weighted,
            jnp.where(inside[None, None, :, None], new_weighted, old_weighted),
            start_row,
            2,
        )
    attention = (
        (weighted / totals[..., None])
        .transpose(2, 0, 1, 3)
        .reshape(tok_count, -1)
        .astype(jnp.bfloat16)
    )
    partial_value = jnp.dot(attention, w_out, preferred_element_type=jnp.float32)
    share_width = hidden_in.shape[1]
    summed = lax.psum(partial_value.astype(jnp.bfloat16), "hid").astype(jnp.float32)
    middle = (whole.astype(jnp.float32) + summed).astype(jnp.bfloat16)
    middle_share = lax.dynamic_slice_in_dim(
        middle, lax.axis_index("hid") * share_width, share_width, 1
    )
    normed_moe = rms_scale(middle, moe_gain)
    local_experts = w_down.shape[0]
    experts = local_experts * req_count
    top_count = routes.shape[1]
    capacity = 2 * tok_count * top_count // experts
    flat_routes, slot = slots_of(routes, experts)
    target = flat_routes * capacity + slot
    token_rows = jnp.repeat(normed_moe, top_count, axis=0)
    outgoing = jnp.zeros((experts * capacity, model_width), jnp.bfloat16).at[target].set(token_rows)
    outgoing = outgoing.reshape(experts, capacity, model_width)
    partial_out = (lambda received: expert_rows(received, w_gate_up, w_down))(
        lax.all_to_all(outgoing, "req", split_axis=0, concat_axis=0, tiled=True)
    )
    reduced = lax.psum_scatter(
        partial_out.astype(jnp.bfloat16), "hid", scatter_dimension=2, tiled=True
    )
    returned = lax.all_to_all(reduced, "req", split_axis=0, concat_axis=0, tiled=True)
    picked = returned.reshape(experts * capacity, -1)[target].reshape(tok_count, top_count, -1)
    expert_sum = jnp.sum(picked.astype(jnp.float32) * gates[:, :, None], axis=1)
    hidden_out = (middle_share.astype(jnp.float32) + expert_sum).astype(jnp.bfloat16)
    return (hidden_out, kv_pages)


def solution(mesh):
    in_specs = (
        P("req", "hid"),
        P("req", None),
        P("req", None),
        P("req", None, "hid", None),
        P("req", None),
        P(),
        P(None, "hid"),
        P(None, "hid"),
        P("hid", None),
        P(),
        P("req", None),
        P("req", None),
        P("req", None, None, "hid"),
        P("req", "hid", None),
    )
    out_specs = (P("req", "hid"), P("req", None, "hid", None))
    return jax.shard_map(shards, mesh=mesh, in_specs=in_specs, out_specs=out_specs, check_vma=False)
```

profile of v0, /device:TPU:0, one launch (start us, length us, event | category | flops | bytes accessed | tf_op | source)
XLA Modules:
  0.0 529.4 jit_solution(13866989351808228242)
XLA Ops:
  7.3 2.5 copy.64
  28.5 4.5 reduce-window.6
  39.7 17.4 %all_gather.6 = bf16[256,1024]{1,0:T(8,128)(2,1)S(1)} all-gather(bf16[256,256]{1,0:T(8,128)(2,1)S(1)} %copy-done.8), channel_id=1, replica_groups=mesh['req'=8,'hid'=4] {'hid'}, dimensions={1}, use_global_device_ids=true | all-gather | bytes 655360 | tf_op jit(solution)/shard_map/all_gather | solution.py:79
  60.3 6.7 %all-gather.2.cloned.1.call-done = bf16[16,1024,2,128]{3,1,2,0:T(8,128)(2,1)} async-done(((bf16[2,1024,2,128]{3,1,2,0:T(8,128)(2,1)}), bf16[16,1024,2,128]{3,1,2,0:T(8,128)(2,1)}) %all-gather.2.cloned.1.call-update) | async-done | bytes 8388624 | tf_op jit(solution)/shard_map/all_gather | solution.py:122
  67.0 3.7 constant_dynamic-slice_fusion.8
  70.7 2.0 copy.79
  72.8 2.1 copy.77
  74.8 2.0 copy.75
  76.8 2.0 copy.73
  87.7 2.1 fusion.50
  96.1 2.1 fusion.49
  98.2 1.8 dynamic_update_slice.73
  105.1 2.1 fusion.48
  113.2 2.1 fusion.47
  121.3 2.1 fusion.46
  125.3 2.9 bitcast_reduce_fusion.2
  128.2 2.1 bitcast_reduce_fusion.1
  131.8 2.1 fusion.31
  135.2 2.1 fusion.45
  141.2 2.1 fusion.44
  149.9 44.7 %all-reduce.2.cloned.1.call-done = bf16[256,1024]{1,0:T(8,128)(2,1)} async-done(((bf16[256,1024]{1,0:T(8,128)(2,1)}), bf16[256,1024]{1,0:T(8,128)(2,1)}) %all-reduce.2.cloned.1.call-update) | async-done | bytes 524304 | tf_op jit(solution)/shard_map/psum | solution.py:173
  196.8 14.6 %scatter_custom_fusion = bf16[4096,1024]{1,0:T(8,128)(2,1)} fusion(s32[2048]{0:T(1024)S(1)} %bitcast.369, bf16[]{:T(256)} %constant.98.clone.1, bf16[256,1024]{1,0:T(8,128)(2,1)S(1)} %fusion.53), kind=kCustom, calls=%fused_computation.8 | custom fusion | bytes 8912898 | tf_op jit(solution)/shard_map/scatter | solution.py:186
  211.4 98.1 %all_to_all.10 = bf16[16,256,1024]{2,1,0:T(8,128)(2,1)S(1)} all-to-all(bf16[16,256,1024]{2,1,0:T(8,128)(2,1)} %bitcast.321), channel_id=1, replica_groups=mesh['req'=8,'hid'=4] {'req'}, dimensions={0} | all-to-all | bytes 16777216 | tf_op jit(solution)/shard_map/all_to_all | solution.py:189
  309.5 3.2 copy-done.2
  312.8 3.7 fusion.2
  316.5 12.7 %convert_bitcast_fusion = bf16[8,2,256,1024]{3,2,0,1:T(8,128)(2,1)} fusion(f32[2,8,256,128]{3,2,1,0:T(8,128)} %fusion.2, bf16[8,2,256,1024]{3,2,1,0:T(8,128)(2,1)} %bitcast.323, bf16[2,128,1024]{2,1,0:T(8,128)(2,1)S(1)} %copy-done, bf16[2,2,1024,128]{3,2,1,0:T(8,128)(2,1)S(1)} %copy-done.35), kind=kOutput, calls=%fused_computation.3 | convolution fusion | flops 2154823680 | bytes 19922944 | tf_op jit(solution)/shard_map/recf,efd->recd/dot_general | solution.py:58
  329.1 7.9 %copy.88 = bf16[8,2,256,1024]{3,2,1,0:T(8,128)(2,1)} copy(bf16[8,2,256,1024]{3,2,0,1:T(8,128)(2,1)} %convert_bitcast_fusion) | data formatting | bytes 16777216 | tf_op jit(solution)/shard_map/convert_element_type | solution.py:192
  337.1 142.7 %reduce-scatter.2.cloned.1.call-done = bf16[16,256,256]{2,1,0:T(8,128)(2,1)} async-done(((bf16[16,256,1024]{2,1,0:T(8,128)(2,1)}), bf16[16,256,256]{2,1,0:T(8,128)(2,1)}) %reduce-scatter.2.cloned.1.call-update) | async-done | bytes 2097168 | tf_op jit(solution)/shard_map/reduce_scatter | solution.py:191
  479.9 3.7 all-to-all-start.1
  486.3 23.9 %all-to-all-done.1 = bf16[16,256,256]{2,1,0:T(8,128)(2,1)S(1)} async-done(((bf16[16,256,256]{2,1,0:T(8,128)(2,1)}), bf16[16,256,256]{2,1,0:T(8,128)(2,1)S(1)}, u32[]{:S(2)}, u32[]{:S(2)}) %all-to-all-start.1) | async-done | bytes 2097184 | tf_op jit(solution)/shard_map/all_to_all | solution.py:194
  510.1 9.0 %gather_fusion = bf16[2048,256]{1,0:T(8,128)(2,1)} fusion(bf16[4096,256]{1,0:T(8,128)(2,1)S(1)} %bitcast.319, s32[2048]{0:T(1024)S(1)} %broadcast_clamp_fusion), kind=kCustom, calls=%fused_computation | custom fusion | bytes 2105344 | tf_op jit(solution)/shard_map/gather | solution.py:195
  519.1 1.9 fusion.7
  (186 shorter events, 61.4 us)
Async XLA Ops:
  7.2 309.3 %copy-start = (bf16[2,128,1024]{2,1,0:T(8,128)(2,1)S(1)}, bf16[2,128,1024]{2,1,0:T(8,128)(2,1)}, u32[]{:S(2)}) copy-start(bf16[2,128,1024]{2,1,0:T(8,128)(2,1)} %param.27) | copy-start | bytes 1572868
  7.2 2.7 copy-start.17
  7.2 13.6 %copy-start.13 = (s32[1,256]{1,0:T(1,128)S(1)}, s32[1,256]{1,0:T(1,128)}, u32[]{:S(2)}) copy-start(s32[1,256]{1,0:T(1,128)} %param.15) | copy-start | bytes 3076
  7.2 19.5 %copy-start.16 = (s32[256,8]{0,1:T(8,128)S(1)}, s32[256,8]{0,1:T(8,128)}, u32[]{:S(2)}) copy-start(s32[256,8]{0,1:T(8,128)} %param.24) | copy-start | bytes 24580
  7.2 32.5 %copy-start.8 = (bf16[256,256]{1,0:T(8,128)(2,1)S(1)}, bf16[256,256]{1,0:T(8,128)(2,1)}, u32[]{:S(2)}) copy-start(bf16[256,256]{1,0:T(8,128)(2,1)} %param.14) | copy-start | bytes 393220
  7.2 59.8 %all-gather.2.cloned.1.call-start = ((), (), s32[]{:S(2)}) async-start(), calls=%async_computation.3 | async-start | bytes 9437184 | tf_op jit(solution)/shard_map/all_gather | solution.py:122
  9.8 47.8 %copy-start.36 = (bf16[1024,256]{1,0:T(8,128)(2,1)S(1)}, bf16[1024,256]{1,0:T(8,128)(2,1)}, u32[]{:S(2)}) copy-start(bf16[1024,256]{1,0:T(8,128)(2,1)} %param.21) | copy-start | bytes 1572868
  9.8 47.8 %copy-start.38 = (f32[1024]{0:T(1024)S(1)}, f32[1024]{0:T(1024)}, u32[]{:S(2)}) copy-start(f32[1024]{0:T(1024)} %param.19) | copy-start | bytes 12292
  9.8 184.7 %all-reduce.2.cloned.1.call-start = ((), (), s32[]{:S(2)}) async-start(), calls=%async_computation.4 | async-start | bytes 1048576 | tf_op jit(solution)/shard_map/psum | solution.py:173
  26.9 31.3 %copy-start.37 = (bf16[1024,256]{1,0:T(8,128)(2,1)S(1)}, bf16[1024,256]{1,0:T(8,128)(2,1)}, u32[]{:S(2)}) copy-start(bf16[1024,256]{1,0:T(8,128)(2,1)} %param.20) | copy-start | bytes 1572868
  39.6 44.9 %copy-start.29 = (pred[128]{0:T(512)(128)(4,1)}, pred[128]{0:T(512)(128)(4,1)S(1)}, u32[]{:S(2)}) copy-start(pred[128]{0:T(512)(128)(4,1)S(1)} %get-tuple-element.68) | copy-start | bytes 388
  89.8 3.5 copy-start.27
  91.8 2.6 copy-start.28
  98.2 4.4 copy-start.25
  101.1 2.6 copy-start.26
  107.2 3.5 copy-start.23
  109.1 2.6 copy-start.24
  115.3 3.5 copy-start.21
  117.2 2.6 copy-start.22
  125.3 5.0 copy-start.20
  130.9 2.9 copy-start.18
  131.7 3.5 copy-start.1
  135.2 3.2 copy-start.32
  147.9 48.7 %copy-start.34 = (f32[1024]{0:T(1024)S(1)}, f32[1024]{0:T(1024)}, u32[]{:S(2)}) copy-start(f32[1024]{0:T(1024)} %param.23) | copy-start | bytes 12292
  149.7 330.2 %reduce-scatter.2.cloned.1.call-start = ((), (), s32[]{:S(2)}) async-start(), calls=%async_computation.5 | async-start | bytes 10485760 | tf_op jit(solution)/shard_map/reduce_scatter | solution.py:191
  211.4 101.3 %copy-start.35 = (bf16[2,2,1024,128]{3,2,1,0:T(8,128)(2,1)S(1)}, bf16[2,2,1024,128]{3,2,1,0:T(8,128)(2,1)}, u32[]{:S(2)}) copy-start(bf16[2,2,1024,128]{3,2,1,0:T(8,128)(2,1)} %param.26) | copy-start | bytes 3145732
  309.5 3.2 copy-start.2
  337.1 147.4 %copy-start.31 = (f32[256,8]{0,1:T(8,128)S(1)}, f32[256,8]{0,1:T(8,128)}, u32[]{:S(2)}) copy-start(f32[256,8]{0,1:T(8,128)} %param.25) | copy-start | bytes 24580
  337.1 147.5 %copy-start.10 = (bf16[256,2,32]{0,2,1:T(8,128)(2,1)S(1)}, bf16[256,2,32]{0,2,1:T(8,128)(2,1)}, u32[]{:S(2)}) copy-start(bf16[256,2,32]{0,2,1:T(8,128)(2,1)} %copy-done.9) | copy-start | bytes 98308
  337.1 147.5 %copy-start.12 = (bf16[256,2,32]{0,2,1:T(8,128)(2,1)S(1)}, bf16[256,2,32]{0,2,1:T(8,128)(2,1)}, u32[]{:S(2)}) copy-start(bf16[256,2,32]{0,2,1:T(8,128)(2,1)} %copy-done.11) | copy-start | bytes 98308
  337.1 147.7 %copy-start.39 = (s32[1,2]{1,0:T(1,128)S(1)}, s32[1,2]{1,0:T(1,128)}, u32[]{:S(2)}) copy-start(s32[1,2]{1,0:T(1,128)} %param.18) | copy-start | bytes 28
  479.9 30.3 %all-to-all-start.1 = ((bf16[16,256,256]{2,1,0:T(8,128)(2,1)}), bf16[16,256,256]{2,1,0:T(8,128)(2,1)S(1)}, u32[]{:S(2)}, u32[]{:S(2)}) async-start(bf16[16,256,256]{2,1,0:T(8,128)(2,1)} %reduce-scatter.2.cloned.1.call-done), calls=%async_computation.2 | async-start | bytes 4194304 | tf_op jit(solution)/shard_map/all_to_all | solution.py:194
  (12 other events, 20.0 us)
Sparse Core Ops, SparseCore 0:
  9.9 57.0 all-gather.1
  149.8 44.7 all-reduce.1
  337.2 142.6 reduce-scatter.1
where the time goes:
time: 536 us; the launch traced here: 529 us
  waiting for transfers between devices  218 us (41%)
  blocking collectives  115 us (21%)
  local copies, waits for them, and re-layouts  80.7 us (15%)
  matrix products  48.3 us (9%)
  between operations  35.4 us (7%)
  other arithmetic  27.8 us (5%)
    reduce_scatter x1, waiting for transfers between devices, shards(): lax.psum_scatter(partial_out.astype(jnp.bfloat16), 'hid', scatter_dimensi...  143 us
    all_to_all x1, blocking collectives, shards(): lax.all_to_all(outgoing, 'req', split_axis=0, concat_axis=0, tiled=True)  98.1 us
    psum x1, waiting for transfers between devices, shards(): lax.psum(partial_value.astype(jnp.bfloat16), 'hid').astype(jnp.float32)  44.7 us
    all_to_all x1, waiting for transfers between devices, shards(): lax.all_to_all(reduced, 'req', split_axis=0, concat_axis=0, tiled=True)  23.9 us
    all_gather x1, blocking collectives, shards(): whole = lax.all_gather(hidden_in, 'hid', axis=1, tiled=True)  17.4 us
    dynamic_slice x9, local copies, waits for them, and re-layouts, shards(): lax.dynamic_index_in_dim(gathered, prefix_group[0, seg], 0, keepdims=False)  16 us
    dot_general x8, matrix products, shards(): jnp.einsum('kgts,skd->kgtd', fresh.astype(jnp.bfloat16), chosen[..., head...  15.1 us
    scatter x1, local copies, waits for them, and re-layouts, shards(): jnp.zeros((experts * capacity, model_width), jnp.bfloat16).at[target]  14.6 us
  transfers between devices with their start and end apart: 4, of which 4 were waited for; matrix products, arithmetic and copies ran while one was open for 3% of the time, Pallas kernels for 0%

commit v1 on v0

--- a/solution.py
+++ b/solution.py
@@ -6,6 +6,18 @@
 PAGE = 128
 EPSILON = 1e-06
 THETA = 10000.0
+
+
+def cut_along(x, dim, count):
+    dims = x.shape
+    blocks = x.reshape(*dims[:dim], count, dims[dim] // count, *dims[dim + 1 :])
+    return jnp.moveaxis(blocks, dim, 0)
+
+
+def joined_along(pieces, dim):
+    pieces = jnp.moveaxis(pieces, 0, dim)
+    shape = pieces.shape
+    return pieces.reshape(*shape[:dim], shape[dim] * shape[dim + 1], *shape[dim + 2 :])
 
 
 def rms_scale(row_data, gain_row):
@@ -191,7 +203,14 @@
     reduced = lax.psum_scatter(
         partial_out.astype(jnp.bfloat16), "hid", scatter_dimension=2, tiled=True
     )
-    returned = lax.all_to_all(reduced, "req", split_axis=0, concat_axis=0, tiled=True)
+    length, place = (lax.axis_size("req"), lax.axis_index("req"))
+    pieces = cut_along(reduced, 0, length)
+    done = [pieces[place]]
+    for lap in range(1, length):
+        sent = pieces[(place + lap) % length]
+        done.append(lax.ppermute(sent, "req", [(i, (i + lap) % length) for i in range(length)]))
+    pieces = jnp.stack(done)[(place - jnp.arange(length)) % length]
+    returned = joined_along(pieces, 0)
     picked = returned.reshape(experts * capacity, -1)[target].reshape(tok_count, top_count, -1)
     expert_sum = jnp.sum(picked.astype(jnp.float32) * gates[:, :, None], axis=1)
     hidden_out = (middle_share.astype(jnp.float32) + expert_sum).astype(jnp.bfloat16)

time: 536 us -> 546 us (1.019)
  the two profiles are of different devices: /device:TPU:0 before, /device:TPU:19 now
where the time goes in v1:
time: 546 us; the launch traced here: 539 us
  waiting for transfers between devices  210 us (38%)
  blocking collectives  112 us (21%)
  local copies, waits for them, and re-layouts  97 us (18%)
  matrix products  48.2 us (9%)
  between operations  35.5 us (7%)
  other arithmetic  27.8 us (5%)
  starting transfers between devices  7.56 us (1%)
    reduce_scatter x1, waiting for transfers between devices, shards(): lax.psum_scatter(partial_out.astype(jnp.bfloat16), 'hid', scatter_dimensi...  144 us
    all_to_all x1, blocking collectives, shards(): lax.all_to_all(outgoing, 'req', split_axis=0, concat_axis=0, tiled=True)  99.3 us
    psum x1, waiting for transfers between devices, shards(): lax.psum(partial_value.astype(jnp.bfloat16), 'hid').astype(jnp.float32)  35.8 us
    ppermute x7, waiting for transfers between devices, shards(): lax.ppermute(sent, 'req', [(i, (i + lap) % length) for i in range(length)])  20.7 us
    dynamic_slice x9, local copies, waits for them, and re-layouts, shards(): lax.dynamic_index_in_dim(gathered, prefix_group[0, seg], 0, keepdims=False)  16 us
    dot_general x8, matrix products, shards(): jnp.einsum('kgts,skd->kgtd', fresh.astype(jnp.bfloat16), chosen[..., head...  15.1 us
    scatter x1, local copies, waits for them, and re-layouts, shards(): jnp.zeros((experts * capacity, model_width), jnp.bfloat16).at[target]  14.6 us
    dot_general x8, matrix products, shards(): jnp.einsum('tkgd,skd->kgts', query_window, chosen[..., :head_dim], prefer...  14.1 us
  transfers between devices with their start and end apart: 10, of which 6 were waited for; matrix products, arithmetic and copies ran while one was open for 4% of the time, Pallas kernels for 0%

profile of v1, /device:TPU:19, one launch (start us, length us, event | category | flops | bytes accessed | tf_op | source)
XLA Modules:
  0.0 538.6 jit_solution(4998497795187786395)
XLA Ops:
  7.3 2.5 copy.64
  28.5 4.5 reduce-window.6
  39.7 12.9 %all_gather.6 = bf16[256,1024]{1,0:T(8,128)(2,1)S(1)} all-gather(bf16[256,256]{1,0:T(8,128)(2,1)S(1)} %copy-done.8), channel_id=1, replica_groups=mesh['req'=8,'hid'=4] {'hid'}, dimensions={1}, use_global_device_ids=true | all-gather | bytes 655360 | tf_op jit(solution)/shard_map/all_gather | solution.py:91
  55.8 9.9 %all-gather.2.cloned.1.call-done = bf16[16,1024,2,128]{3,1,2,0:T(8,128)(2,1)} async-done(((bf16[2,1024,2,128]{3,1,2,0:T(8,128)(2,1)}), bf16[16,1024,2,128]{3,1,2,0:T(8,128)(2,1)}) %all-gather.2.cloned.1.call-update) | async-done | bytes 8388624 | tf_op jit(solution)/shard_map/all_gather | solution.py:134
  65.7 3.7 constant_dynamic-slice_fusion.8
  69.5 2.0 copy.79
  71.5 2.1 copy.77
  73.6 2.0 copy.75
  86.5 2.1 fusion.50
  94.9 2.1 fusion.49
  104.1 2.1 fusion.48
  113.4 2.1 fusion.47
  122.7 2.1 fusion.46
  127.7 2.9 bitcast_reduce_fusion.2
  130.6 2.1 bitcast_reduce_fusion.1
  134.4 2.1 fusion.31
  137.9 2.1 fusion.45
  145.1 2.1 fusion.44
  154.7 35.8 %all-reduce.2.cloned.1.call-done = bf16[256,1024]{1,0:T(8,128)(2,1)} async-done(((bf16[256,1024]{1,0:T(8,128)(2,1)}), bf16[256,1024]{1,0:T(8,128)(2,1)}) %all-reduce.2.cloned.1.call-update) | async-done | bytes 524304 | tf_op jit(solution)/shard_map/psum | solution.py:185
  192.7 14.6 %scatter_custom_fusion = bf16[4096,1024]{1,0:T(8,128)(2,1)} fusion(s32[2048]{0:T(1024)S(1)} %bitcast.400, bf16[]{:T(256)} %constant.152.clone.1, bf16[256,1024]{1,0:T(8,128)(2,1)S(1)} %fusion.53), kind=kCustom, calls=%fused_computation.9 | custom fusion | bytes 8912898 | tf_op jit(solution)/shard_map/scatter | solution.py:198
  207.3 99.3 %all_to_all.5 = bf16[16,256,1024]{2,1,0:T(8,128)(2,1)S(1)} all-to-all(bf16[16,256,1024]{2,1,0:T(8,128)(2,1)} %bitcast.352), channel_id=1, replica_groups=mesh['req'=8,'hid'=4] {'req'}, dimensions={0} | all-to-all | bytes 16777216 | tf_op jit(solution)/shard_map/all_to_all | solution.py:201
  306.6 3.2 copy-done.2
  309.8 3.7 fusion.2
  313.5 12.7 %convert_bitcast_fusion = bf16[8,2,256,1024]{3,2,0,1:T(8,128)(2,1)} fusion(f32[2,8,256,128]{3,2,1,0:T(8,128)} %fusion.2, bf16[8,2,256,1024]{3,2,1,0:T(8,128)(2,1)} %bitcast.354, bf16[2,128,1024]{2,1,0:T(8,128)(2,1)S(1)} %copy-done, bf16[2,2,1024,128]{3,2,1,0:T(8,128)(2,1)S(1)} %copy-done.35), kind=kOutput, calls=%fused_computation.4 | convolution fusion | flops 2154823680 | bytes 19922944 | tf_op jit(solution)/shard_map/recf,efd->recd/dot_general | solution.py:70
  326.2 7.9 %copy.88 = bf16[8,2,256,1024]{3,2,1,0:T(8,128)(2,1)} copy(bf16[8,2,256,1024]{3,2,0,1:T(8,128)(2,1)} %convert_bitcast_fusion) | data formatting | bytes 16777216 | tf_op jit(solution)/shard_map/convert_element_type | solution.py:204
  334.8 144.0 %reduce-scatter.2.cloned.1.call-done = bf16[16,256,256]{2,1,0:T(8,128)(2,1)} async-done(((bf16[16,256,1024]{2,1,0:T(8,128)(2,1)}), bf16[16,256,256]{2,1,0:T(8,128)(2,1)}) %reduce-scatter.2.cloned.1.call-update) | async-done | bytes 2097168 | tf_op jit(solution)/shard_map/reduce_scatter | solution.py:203
  478.8 2.3 dynamic-slice_bitcast_fusion
  490.8 3.3 collective-permute-done.1
  496.0 11.5 %collective-permute-done.2 = bf16[2,256,256]{2,1,0:T(8,128)(2,1)S(1)} collective-permute-done((bf16[2,256,256]{2,1,0:T(8,128)(2,1)S(1)}, bf16[2,256,256]{2,1,0:T(8,128)(2,1)S(1)}, u32[]{:S(2)}, u32[]{:S(2)}) %collective-permute-start.2) | collective-permute-done | bytes 262176 | tf_op jit(solution)/shard_map/ppermute | solution.py:211
  508.2 5.9 %collective-permute-done.3 = bf16[2,256,256]{2,1,0:T(8,128)(2,1)S(1)} collective-permute-done((bf16[2,256,256]{2,1,0:T(8,128)(2,1)S(1)}, bf16[2,256,256]{2,1,0:T(8,128)(2,1)S(1)}, u32[]{:S(2)}, u32[]{:S(2)}) %collective-permute-start.3) | collective-permute-done | bytes 262176 | tf_op jit(solution)/shard_map/ppermute | solution.py:211
  517.0 2.3 gather_fusion
  519.3 9.0 %gather_fusion.1 = bf16[2048,256]{1,0:T(8,128)(2,1)} fusion(bf16[4096,256]{1,0:T(8,128)(2,1)S(1)} %bitcast.350, s32[2048]{0:T(1024)S(1)} %broadcast_clamp_fusion), kind=kCustom, calls=%fused_computation.1 | custom fusion | bytes 2105344 | tf_op jit(solution)/shard_map/gather | solution.py:214
  (209 shorter events, 86.3 us)
Async XLA Ops:
  7.2 306.3 %copy-start = (bf16[2,128,1024]{2,1,0:T(8,128)(2,1)S(1)}, bf16[2,128,1024]{2,1,0:T(8,128)(2,1)}, u32[]{:S(2)}) copy-start(bf16[2,128,1024]{2,1,0:T(8,128)(2,1)} %param.27) | copy-start | bytes 1572868
  7.2 13.6 %copy-start.13 = (s32[1,256]{1,0:T(1,128)S(1)}, s32[1,256]{1,0:T(1,128)}, u32[]{:S(2)}) copy-start(s32[1,256]{1,0:T(1,128)} %param.15) | copy-start | bytes 3076
  7.2 19.5 %copy-start.16 = (s32[256,8]{0,1:T(8,128)S(1)}, s32[256,8]{0,1:T(8,128)}, u32[]{:S(2)}) copy-start(s32[256,8]{0,1:T(8,128)} %param.24) | copy-start | bytes 24580
  7.2 32.5 %copy-start.8 = (bf16[256,256]{1,0:T(8,128)(2,1)S(1)}, bf16[256,256]{1,0:T(8,128)(2,1)}, u32[]{:S(2)}) copy-start(bf16[256,256]{1,0:T(8,128)(2,1)} %param.14) | copy-start | bytes 393220
  7.2 58.5 %all-gather.2.cloned.1.call-start = ((), (), s32[]{:S(2)}) async-start(), calls=%async_computation.2 | async-start | bytes 9437184 | tf_op jit(solution)/shard_map/all_gather | solution.py:134
  9.8 43.3 %copy-start.36 = (bf16[1024,256]{1,0:T(8,128)(2,1)S(1)}, bf16[1024,256]{1,0:T(8,128)(2,1)}, u32[]{:S(2)}) copy-start(bf16[1024,256]{1,0:T(8,128)(2,1)} %param.21) | copy-start | bytes 1572868
  9.8 43.3 %copy-start.38 = (f32[1024]{0:T(1024)S(1)}, f32[1024]{0:T(1024)}, u32[]{:S(2)}) copy-start(f32[1024]{0:T(1024)} %param.19) | copy-start | bytes 12292
  9.8 180.6 %all-reduce.2.cloned.1.call-start = ((), (), s32[]{:S(2)}) async-start(), calls=%async_computation.3 | async-start | bytes 1048576 | tf_op jit(solution)/shard_map/psum | solution.py:185
  26.9 26.8 %copy-start.37 = (bf16[1024,256]{1,0:T(8,128)(2,1)S(1)}, bf16[1024,256]{1,0:T(8,128)(2,1)}, u32[]{:S(2)}) copy-start(bf16[1024,256]{1,0:T(8,128)(2,1)} %param.20) | copy-start | bytes 1572868
  39.6 43.7 %copy-start.29 = (pred[128]{0:T(512)(128)(4,1)}, pred[128]{0:T(512)(128)(4,1)S(1)}, u32[]{:S(2)}) copy-start(pred[128]{0:T(512)(128)(4,1)S(1)} %get-tuple-element.76) | copy-start | bytes 388
  88.6 3.5 copy-start.27
  96.9 4.4 copy-start.25
  106.2 4.4 copy-start.23
  115.5 4.4 copy-start.21
  127.7 5.0 copy-start.20
  133.3 3.2 copy-start.18
  134.4 3.5 copy-start.1
  137.9 3.9 copy-start.32
  152.8 39.8 %copy-start.34 = (f32[1024]{0:T(1024)S(1)}, f32[1024]{0:T(1024)}, u32[]{:S(2)}) copy-start(f32[1024]{0:T(1024)} %param.23) | copy-start | bytes 12292
  154.5 324.2 %reduce-scatter.2.cloned.1.call-start = ((), (), s32[]{:S(2)}) async-start(), calls=%async_computation.4 | async-start | bytes 10485760 | tf_op jit(solution)/shard_map/reduce_scatter | solution.py:203
  207.3 102.5 %copy-start.35 = (bf16[2,2,1024,128]{3,2,1,0:T(8,128)(2,1)S(1)}, bf16[2,2,1024,128]{3,2,1,0:T(8,128)(2,1)}, u32[]{:S(2)}) copy-start(bf16[2,2,1024,128]{3,2,1,0:T(8,128)(2,1)} %param.26) | copy-start | bytes 3145732
  306.6 3.2 copy-start.2
  478.7 5.1 copy-start.10
  478.7 5.1 copy-start.12
  478.7 6.4 %copy-start.31 = (f32[256,8]{0,1:T(8,128)S(1)}, f32[256,8]{0,1:T(8,128)}, u32[]{:S(2)}) copy-start(f32[256,8]{0,1:T(8,128)} %param.25) | copy-start | bytes 24580
  481.1 8.1 %collective-permute-start = (bf16[2,256,256]{2,1,0:T(8,128)(2,1)S(1)}, bf16[2,256,256]{2,1,0:T(8,128)(2,1)S(1)}, u32[]{:S(2)}, u32[]{:S(2)}) collective-permute-start(bf16[2,256,256]{2,1,0:T(8,128)(2,1)S(1)} %get-tuple-element.62), channel_id=1, source_target_pairs={{0,4},{4,8},{8,12},{12,16},{16,20},{20,24},{24,28},{28,0},{1,5},{5... | collective-permute-start | bytes 786440 | tf_op jit(solution)/shard_map/ppermute | solution.py:211
  483.9 10.2 %collective-permute-start.1 = (bf16[2,256,256]{2,1,0:T(8,128)(2,1)S(1)}, bf16[2,256,256]{2,1,0:T(8,128)(2,1)S(1)}, u32[]{:S(2)}, u32[]{:S(2)}) collective-permute-start(bf16[2,256,256]{2,1,0:T(8,128)(2,1)S(1)} %get-tuple-element.61), channel_id=1, source_target_pairs={{0,8},{4,12},{8,16},{12,20},{16,24},{20,28},{24,0},{28,4},{1,9},{5... | collective-permute-start | bytes 786440 | tf_op jit(solution)/shard_map/ppermute | solution.py:211
  486.9 29.4 %collective-permute-start.6 = (bf16[2,256,256]{2,1,0:T(8,128)(2,1)S(1)}, bf16[2,256,256]{2,1,0:T(8,128)(2,1)S(1)}, u32[]{:S(2)}, u32[]{:S(2)}) collective-permute-start(bf16[2,256,256]{2,1,0:T(8,128)(2,1)S(1)} %get-tuple-element.56), channel_id=1, source_target_pairs={{0,28},{4,0},{8,4},{12,8},{16,12},{20,16},{24,20},{28,24},{1,29},{... | collective-permute-start | bytes 786440 | tf_op jit(solution)/shard_map/ppermute | solution.py:211
  486.9 28.7 %collective-permute-start.5 = (bf16[2,256,256]{2,1,0:T(8,128)(2,1)S(1)}, bf16[2,256,256]{2,1,0:T(8,128)(2,1)S(1)}, u32[]{:S(2)}, u32[]{:S(2)}) collective-permute-start(bf16[2,256,256]{2,1,0:T(8,128)(2,1)S(1)} %get-tuple-element.57), channel_id=1, source_target_pairs={{0,24},{4,28},{8,0},{12,4},{16,8},{20,12},{24,16},{28,20},{1,25},{... | collective-permute-start | bytes 786440 | tf_op jit(solution)/shard_map/ppermute | solution.py:211
  487.2 27.7 %collective-permute-start.4 = (bf16[2,256,256]{2,1,0:T(8,128)(2,1)S(1)}, bf16[2,256,256]{2,1,0:T(8,128)(2,1)S(1)}, u32[]{:S(2)}, u32[]{:S(2)}) collective-permute-start(bf16[2,256,256]{2,1,0:T(8,128)(2,1)S(1)} %get-tuple-element.58), channel_id=1, source_target_pairs={{0,20},{4,24},{8,28},{12,0},{16,4},{20,8},{24,12},{28,16},{1,21},{... | collective-permute-start | bytes 786440 | tf_op jit(solution)/shard_map/ppermute | solution.py:211
  489.2 18.3 %collective-permute-start.2 = (bf16[2,256,256]{2,1,0:T(8,128)(2,1)S(1)}, bf16[2,256,256]{2,1,0:T(8,128)(2,1)S(1)}, u32[]{:S(2)}, u32[]{:S(2)}) collective-permute-start(bf16[2,256,256]{2,1,0:T(8,128)(2,1)S(1)} %get-tuple-element.60), channel_id=1, source_target_pairs={{0,12},{4,16},{8,20},{12,24},{16,28},{20,0},{24,4},{28,8},{1,13},{... | collective-permute-start | bytes 786440 | tf_op jit(solution)/shard_map/ppermute | solution.py:211
  494.1 20.0 %collective-permute-start.3 = (bf16[2,256,256]{2,1,0:T(8,128)(2,1)S(1)}, bf16[2,256,256]{2,1,0:T(8,128)(2,1)S(1)}, u32[]{:S(2)}, u32[]{:S(2)}) collective-permute-start(bf16[2,256,256]{2,1,0:T(8,128)(2,1)S(1)} %get-tuple-element.59), channel_id=1, source_target_pairs={{0,16},{4,20},{8,24},{12,28},{16,0},{20,4},{24,8},{28,12},{1,17},{... | collective-permute-start | bytes 786440 | tf_op jit(solution)/shard_map/ppermute | solution.py:211
  (18 other events, 33.5 us)
Sparse Core Ops, SparseCore 0:
  9.9 55.7 all-gather.1
  154.6 35.7 all-reduce.1
  334.2 144.4 reduce-scatter.1
